TPU v7x, 256 devices: a whole 4x4x8 slice. The times are simulated.
256 devices in a mesh: shard: 64 (over x, z_hi, y), rep: 4 (over z_lo, core).
Axes of the slice: x: 4, y: 4, z: 8 (z_hi: 4, z_lo: 2; z = z_hi * 2 + z_lo), core: 2. Of those that a mesh axis runs over, the one named last changes fastest.
Arguments:
- docs: bfloat16 [32768, 16384], P('shard', 'rep')
- pattern: int32 [256, 128], P('shard', 'rep'), may hold values 0 or 1
- owners: int32 [4], replicated, may hold values from 0 to 63
Outputs:
- scores: bfloat16 [4, 256, 32768], P(None, ('shard', 'rep'))
All inputs are finite; a program needn't handle non-finite values. No bound on the sum of `pattern` on one device may be relied on, other than what follows from the above.
Results may differ from a plain program's by a relative error of at most 0.001.
Values may be sent and summed in bfloat16 or wider, within the bound.
No kernel may reach another device: no remote copies, remote signals or barrier semaphores. Data moves between devices by JAX's collectives and lax.ppermute only.
A program may use at most 128 MiB of HBM per device.

v0:
```python
import math
import jax
import jax.numpy as jnp
from jax import lax
from jax.sharding import PartitionSpec as P

TERMS = 16384
QUERY = 256
STEPS = 4
EPSILON = 1e-06
CLIP_LEVEL = 1.5


def from_root(block, axis, owner):
    block = jnp.where(lax.axis_index(axis) == owner, block, jnp.zeros_like(block))
    return lax.psum(block, axis)


def on_device(docs, pattern, owners):
    n_shard = lax.axis_size("shard")
    n_rep = lax.axis_size("rep")
    shard_index = lax.axis_index("shard")
    rep_index = lax.axis_index("rep")
    doc_rows, term_cols = docs.shape
    tile_edge = 128
    row_share = QUERY // (n_shard * n_rep)
    weights = pattern.astype(jnp.bfloat16)
    masked = (
        docs.reshape(doc_rows // tile_edge, tile_edge, term_cols // tile_edge, tile_edge)
        * weights[:, None, :, None]
    ).reshape(doc_rows, term_cols)
    partial_sq = jnp.einsum("dt,dt->d", masked, masked, preferred_element_type=jnp.float32)
    doc_sq = lax.psum(partial_sq, "rep")
    inverse = lax.rsqrt(doc_sq + EPSILON)
    all_inverse = lax.all_gather(inverse, "shard", axis=0, tiled=True)
    sharpen = math.sqrt(TERMS) * 0.5
    results = []
    for step_index in range(STEPS):
        offset = step_index % (doc_rows // QUERY) * QUERY
        candidate = masked[offset : offset + QUERY]
        queries = from_root(candidate, "shard", owners[step_index])
        offset = step_index % (doc_rows // QUERY) * QUERY
        first_global = owners[step_index] * doc_rows + offset
        query_inv = lax.dynamic_slice_in_dim(all_inverse, first_global, QUERY, 0).reshape(
            n_shard, n_rep, row_share
        )
        similar = lax.dot_general(
            queries, masked, (((1,), (1,)), ((), ())), preferred_element_type=jnp.float32
        )
        summed = lax.psum(similar, "rep").reshape(n_shard, n_rep, row_share, doc_rows)
        own_rows = lax.dynamic_index_in_dim(summed, rep_index, 1, keepdims=False)
        received = lax.all_to_all(own_rows, "shard", split_axis=0, concat_axis=2, tiled=True)[0]
        shard_inv = lax.dynamic_index_in_dim(query_inv, shard_index, 0, keepdims=False)
        row_inv = lax.dynamic_index_in_dim(shard_inv, rep_index, 0, keepdims=False)
        scaled = received * row_inv[:, None] * all_inverse[None, :] * sharpen
        results.append(jnp.clip(scaled, -CLIP_LEVEL, CLIP_LEVEL).astype(jnp.bfloat16))
    return jnp.stack(results)


def solution(mesh):
    return jax.shard_map(
        on_device,
        mesh=mesh,
        in_specs=(P("shard", "rep"), P("shard", "rep"), P()),
        out_specs=P(None, ("shard", "rep"), None),
        check_vma=False,
    )
```

profile of v0, /device:TPU:32, one launch (start us, length us, event | category | flops | bytes accessed | tf_op | source)
XLA Modules:
  0.0 1161.1 jit_solution(10522000148827303313)
XLA Ops:
  11.1 3.4 copy.8
  15.5 6.0 copy_bitcast_fusion.2
  21.6 6.0 copy_bitcast_fusion
  28.5 1.6 copy-done
  30.0 3.7 fusion
  33.8 771.8 %all-reduce.7.cloned.1.call-done = (bf16[256,4096]{1,0:T(8,128)(2,1)}, bf16[256,4096]{1,0:T(8,128)(2,1)}, bf16[256,4096]{1,0:T(8,128)(2,1)}, bf16[256,4096]{1,0:T(8,128)(2,1)}) async-done(((bf16[256,4096]{1,0:T(8,128)(2,1)}, bf16[256,4096]{1,0:T(8,128)(2,1)}, bf16[256,4096]{1,0:T(8,128)(2,1)}, bf16[256,4096]{1,0:T(8,128)(2,1)}), (bf16[256,4096]{1,0:T(8,128)(2,1)}, bf16[256,4096]{1,0:T(8,128)(2,1)}, ...) | async-done | bytes 8388624 | tf_op jit(solution)/shard_map/psum | solution.py:16
  805.5 4.2 fusion.3
  810.7 3.8 fusion.4
  815.5 4.3 fusion.5
  820.8 3.8 fusion.6
  825.6 7.8 psum.65
  833.3 52.9 %all-reduce.5.cloned.1.call-done = (f32[64,4,1,512]{3,1,0,2:T(4,128)}, f32[64,4,1,512]{3,1,0,2:T(4,128)}, f32[64,4,1,512]{3,1,0,2:T(4,128)}, f32[64,4,1,512]{3,1,0,2:T(4,128)}) async-done(((f32[64,4,1,512]{3,1,0,2:T(4,128)}, f32[64,4,1,512]{3,1,0,2:T(4,128)}, f32[64,4,1,512]{3,1,0,2:T(4,128)}, f32[64,4,1,512]{3,1,0,2:T(4,128)}), (f32[64,4,1,512]{3,1,0,2:T(4,128)}, f32[64,4,1,512]{3,1,0,2:T(4,128)}, ...) | async-done | bytes 2097168 | tf_op jit(solution)/shard_map/psum | solution.py:50
  886.2 1.8 dynamic-slice_bitcast_fusion.2
  888.0 13.1 %all-to-all-start.1 = ((f32[64,1,512]{2,1,0:T(1,128)}), f32[64,1,512]{2,1,0:T(1,128)S(1)}, u32[]{:S(2)}, u32[]{:S(2)}) async-start(f32[64,1,512]{2,1,0:T(1,128)} %dynamic-slice_bitcast_fusion.2), calls=%async_computation.1 | async-start | bytes 262144 | tf_op jit(solution)/shard_map/all_to_all | solution.py:52
  901.2 1.8 dynamic-slice_bitcast_fusion.1
  903.0 11.3 all-to-all-done.1
  914.3 4.6 all-to-all-start.2
  918.9 192.4 %all-gather = f32[64,1,512]{2,1,0:T(1,128)S(1)} all-gather(f32[1,1,512]{2,1,0:T(1,128)S(1)} %bitcast.81), channel_id=1, replica_groups=mesh['shard'=64,'rep'=4] {'shard'}, dimensions={0}, use_global_device_ids=true | all-gather | bytes 133120 | tf_op jit(solution)/shard_map/all_gather | solution.py:35
  1115.6 1.8 dynamic-slice_bitcast_fusion
  1117.4 4.6 all-to-all-start.3
  1122.1 1.8 dynamic-slice_bitcast_fusion.3
  1124.5 10.1 all-to-all-done.3
  1134.7 4.6 all-to-all-start
  1140.5 11.4 all-to-all-done
  (37 shorter events, 13.7 us)
Async XLA Ops:
  6.5 799.0 %all-reduce.7.cloned.1.call-start = ((), (), s32[]{:S(2)}) async-start(), calls=%async_computation.5 | async-start | bytes 16777216 | tf_op jit(solution)/shard_map/psum | solution.py:16
  27.6 858.6 %all-reduce.5.cloned.1.call-start = ((), (), s32[]{:S(2)}) async-start(), calls=%async_computation.4 | async-start | bytes 4194304 | tf_op jit(solution)/shard_map/psum | solution.py:50
  27.8 2.2 copy-start
  805.5 5.2 copy-start.2
  815.5 5.2 copy-start.1
  888.0 26.2 %all-to-all-start.1 = ((f32[64,1,512]{2,1,0:T(1,128)}), f32[64,1,512]{2,1,0:T(1,128)S(1)}, u32[]{:S(2)}, u32[]{:S(2)}) async-start(f32[64,1,512]{2,1,0:T(1,128)} %dynamic-slice_bitcast_fusion.2), calls=%async_computation.1 | async-start | bytes 262144 | tf_op jit(solution)/shard_map/all_to_all | solution.py:52
  914.3 203.2 %all-to-all-start.2 = ((f32[64,1,512]{2,1,0:T(1,128)}), f32[64,1,512]{2,1,0:T(1,128)S(1)}, u32[]{:S(2)}, u32[]{:S(2)}) async-start(f32[64,1,512]{2,1,0:T(1,128)} %dynamic-slice_bitcast_fusion.1), calls=%async_computation.2 | async-start | bytes 262144 | tf_op jit(solution)/shard_map/all_to_all | solution.py:52
  1117.4 17.2 %all-to-all-start.3 = ((f32[64,1,512]{2,1,0:T(1,128)}), f32[64,1,512]{2,1,0:T(1,128)S(1)}, u32[]{:S(2)}, u32[]{:S(2)}) async-start(f32[64,1,512]{2,1,0:T(1,128)} %dynamic-slice_bitcast_fusion), calls=%async_computation.3 | async-start | bytes 262144 | tf_op jit(solution)/shard_map/all_to_all | solution.py:52
  1134.7 17.2 %all-to-all-start = ((f32[64,1,512]{2,1,0:T(1,128)}), f32[64,1,512]{2,1,0:T(1,128)S(1)}, u32[]{:S(2)}, u32[]{:S(2)}) async-start(f32[64,1,512]{2,1,0:T(1,128)} %dynamic-slice_bitcast_fusion.3), calls=%async_computation | async-start | bytes 262144 | tf_op jit(solution)/shard_map/all_to_all | solution.py:52
Sparse Core Ops, SparseCore 0:
  27.7 777.7 all-reduce.6
  825.7 60.4 all-reduce.4
where the time goes:
time: 1160 us
  waiting for transfers between devices  857 us (74%)
  blocking collectives  200 us (17%)
  local copies, waits for them, and re-layouts  32.3 us (3%)
  starting transfers between devices  27.2 us (2%)
  between operations  18.5 us (2%)
  matrix products  16.1 us (1%)
    psum x1, waiting for transfers between devices, from_root(): return lax.psum(block, axis)  772 us
    all_gather x1, blocking collectives, on_device(): all_inverse = lax.all_gather(inverse, 'shard', axis=0, tiled=True)  192 us
    psum x1, waiting for transfers between devices, on_device(): lax.psum(similar, 'rep').reshape(n_shard, n_rep, row_share, doc_rows)  52.9 us
    all_to_all x4, waiting for transfers between devices, on_device(): lax.all_to_all(own_rows, 'shard', split_axis=0, concat_axis=2, tiled=True)  32.8 us
    all_to_all x4, starting transfers between devices, on_device(): lax.all_to_all(own_rows, 'shard', split_axis=0, concat_axis=2, tiled=True)  27 us
  transfers between devices with their start and end apart: 6, of which 5 were waited for; matrix products, arithmetic and copies ran while one was open for 1% of the time, Pallas kernels for 0%

commit v1 on v0

--- a/solution.py
+++ b/solution.py
@@ -47,7 +47,9 @@
         similar = lax.dot_general(
             queries, masked, (((1,), (1,)), ((), ())), preferred_element_type=jnp.float32
         )
-        summed = lax.psum(similar, "rep").reshape(n_shard, n_rep, row_share, doc_rows)
+        summed = jnp.sum(lax.all_gather(similar, "rep"), axis=0).reshape(
+            n_shard, n_rep, row_share, doc_rows
+        )
         own_rows = lax.dynamic_index_in_dim(summed, rep_index, 1, keepdims=False)
         received = lax.all_to_all(own_rows, "shard", split_axis=0, concat_axis=2, tiled=True)[0]
         shard_inv = lax.dynamic_index_in_dim(query_inv, shard_index, 0, keepdims=False)

time: 1160 us -> 1140 us (0.983)
  waiting for transfers between devices: 857 us -> 823 us
    psum x1 -> x0, waiting for transfers between devices: 52.9 us -> none  [on_device(): lax.psum(similar, 'rep').reshape(n_shard, n_rep, row_share, doc_rows)]
    all_gather x0 -> x4, waiting for transfers between devices: none -> 28.6 us  [on_device(): lax.all_gather(similar, 'rep')]
  transfers between devices with their start and end apart: 6 -> 9, of which waited for: 5 -> 5; matrix products, arithmetic and copies ran while one was open for 1% -> 3% of each run, Pallas kernels for 0% -> 0%
where the time goes in v1:
time: 1140 us
  waiting for transfers between devices  823 us (72%)
  blocking collectives  201 us (18%)
  starting transfers between devices  35.8 us (3%)
  local copies, waits for them, and re-layouts  25 us (2%)
  matrix products  19.5 us (2%)
  between operations  18.4 us (2%)
  other arithmetic  16.8 us (1%)
    psum x1, waiting for transfers between devices, from_root(): return lax.psum(block, axis)  772 us
    all_gather x1, blocking collectives, on_device(): all_inverse = lax.all_gather(inverse, 'shard', axis=0, tiled=True)  193 us
    all_to_all x4, starting transfers between devices, on_device(): lax.all_to_all(own_rows, 'shard', split_axis=0, concat_axis=2, tiled=True)  35.4 us
    all_gather x4, waiting for transfers between devices, on_device(): lax.all_gather(similar, 'rep')  28.6 us
  transfers between devices with their start and end apart: 9, of which 5 were waited for; matrix products, arithmetic and copies ran while one was open for 3% of the time, Pallas kernels for 0%

profile of v1, /device:TPU:32, one launch (start us, length us, event | category | flops | bytes accessed | tf_op | source)
XLA Modules:
  0.0 1139.3 jit_solution(13977109982011696241)
XLA Ops:
  11.1 3.4 copy.8
  15.5 6.1 copy_bitcast_fusion.2
  21.6 6.0 copy_bitcast_fusion
  28.5 1.6 copy-done
  30.1 3.7 fusion
  33.8 771.8 %all-reduce.3.cloned.1.call-done = (bf16[256,4096]{1,0:T(8,128)(2,1)}, bf16[256,4096]{1,0:T(8,128)(2,1)}, bf16[256,4096]{1,0:T(8,128)(2,1)}, bf16[256,4096]{1,0:T(8,128)(2,1)}) async-done(((bf16[256,4096]{1,0:T(8,128)(2,1)}, bf16[256,4096]{1,0:T(8,128)(2,1)}, bf16[256,4096]{1,0:T(8,128)(2,1)}, bf16[256,4096]{1,0:T(8,128)(2,1)}), (bf16[256,4096]{1,0:T(8,128)(2,1)}, bf16[256,4096]{1,0:T(8,128)(2,1)}, ...) | async-done | bytes 8388624 | tf_op jit(solution)/shard_map/psum | solution.py:16
  805.6 5.1 fusion.4
  810.7 4.6 fusion.5
  815.4 5.1 fusion.6
  820.6 4.8 fusion.3
  825.4 7.9 psum.36
  833.3 7.6 all-gather.12.cloned.1.call-done
  840.9 1.9 reduce_sum.37
  843.7 13.1 %all-to-all-start.1 = ((f32[64,1,512]{2,1,0:T(1,128)}), f32[64,1,512]{2,1,0:T(1,128)S(1)}, u32[]{:S(2)}, u32[]{:S(2)}) async-start(f32[64,1,512]{2,1,0:T(1,128)} %dynamic-slice_bitcast_fusion.2), calls=%async_computation.1 | async-start | bytes 262144 | tf_op jit(solution)/shard_map/all_to_all | solution.py:54
  856.9 21.0 %all-gather.14.cloned.1.call-done = f32[1024,512]{1,0:T(8,128)} async-done(((f32[256,512]{1,0:T(8,128)}), f32[1024,512]{1,0:T(8,128)}) %all-gather.14.cloned.1.call-update) | async-done | bytes 2097168 | tf_op jit(solution)/shard_map/all_gather | solution.py:50
  877.8 1.9 reduce_sum.38
  880.6 12.9 %all-to-all-start.2 = ((f32[64,1,512]{2,1,0:T(1,128)}), f32[64,1,512]{2,1,0:T(1,128)S(1)}, u32[]{:S(2)}, u32[]{:S(2)}) async-start(f32[64,1,512]{2,1,0:T(1,128)} %dynamic-slice_bitcast_fusion.1), calls=%async_computation.2 | async-start | bytes 262144 | tf_op jit(solution)/shard_map/all_to_all | solution.py:54
  893.5 193.0 %all-gather.4 = f32[64,1,512]{2,1,0:T(1,128)S(1)} all-gather(f32[1,1,512]{2,1,0:T(1,128)S(1)} %bitcast.89), channel_id=1, replica_groups=mesh['shard'=64,'rep'=4] {'shard'}, dimensions={0}, use_global_device_ids=true | all-gather | bytes 133120 | tf_op jit(solution)/shard_map/all_gather | solution.py:35
  1090.9 1.9 reduce_sum.39
  1092.9 1.9 reduce_sum.36
  1095.7 4.8 all-to-all-start.3
  1102.1 11.1 all-to-all-done.3
  1113.2 4.6 all-to-all-start
  1119.1 11.3 all-to-all-done
  (50 shorter events, 13.9 us)
Async XLA Ops:
  6.5 799.0 %all-reduce.3.cloned.1.call-start = ((), (), s32[]{:S(2)}) async-start(), calls=%async_computation.8 | async-start | bytes 16777216 | tf_op jit(solution)/shard_map/psum | solution.py:16
  27.7 813.2 %all-gather.12.cloned.1.call-start = ((), (), s32[]{:S(2)}) async-start(), calls=%async_computation.5 | async-start | bytes 2621440 | tf_op jit(solution)/shard_map/all_gather | solution.py:50
  27.9 2.2 copy-start
  805.6 5.1 copy-start.2
  810.7 67.2 %all-gather.14.cloned.1.call-start = ((), (), s32[]{:S(2)}) async-start(), calls=%async_computation.6 | async-start | bytes 2621440 | tf_op jit(solution)/shard_map/all_gather | solution.py:50
  815.4 275.5 %all-gather.16.cloned.1.call-start = ((), (), s32[]{:S(2)}) async-start(), calls=%async_computation.7 | async-start | bytes 2621440 | tf_op jit(solution)/shard_map/all_gather | solution.py:50
  815.4 5.2 copy-start.1
  820.5 272.4 %all-gather.10.cloned.1.call-start = ((), (), s32[]{:S(2)}) async-start(), calls=%async_computation.4 | async-start | bytes 2621440 | tf_op jit(solution)/shard_map/all_gather | solution.py:50
  843.7 36.9 %all-to-all-start.1 = ((f32[64,1,512]{2,1,0:T(1,128)}), f32[64,1,512]{2,1,0:T(1,128)S(1)}, u32[]{:S(2)}, u32[]{:S(2)}) async-start(f32[64,1,512]{2,1,0:T(1,128)} %dynamic-slice_bitcast_fusion.2), calls=%async_computation.1 | async-start | bytes 262144 | tf_op jit(solution)/shard_map/all_to_all | solution.py:54
  880.6 215.1 %all-to-all-start.2 = ((f32[64,1,512]{2,1,0:T(1,128)}), f32[64,1,512]{2,1,0:T(1,128)S(1)}, u32[]{:S(2)}, u32[]{:S(2)}) async-start(f32[64,1,512]{2,1,0:T(1,128)} %dynamic-slice_bitcast_fusion.1), calls=%async_computation.2 | async-start | bytes 262144 | tf_op jit(solution)/shard_map/all_to_all | solution.py:54
  1095.7 17.4 %all-to-all-start.3 = ((f32[64,1,512]{2,1,0:T(1,128)}), f32[64,1,512]{2,1,0:T(1,128)S(1)}, u32[]{:S(2)}, u32[]{:S(2)}) async-start(f32[64,1,512]{2,1,0:T(1,128)} %dynamic-slice_bitcast_fusion), calls=%async_computation.3 | async-start | bytes 262144 | tf_op jit(solution)/shard_map/all_to_all | solution.py:54
  1113.2 17.2 %all-to-all-start = ((f32[64,1,512]{2,1,0:T(1,128)}), f32[64,1,512]{2,1,0:T(1,128)S(1)}, u32[]{:S(2)}, u32[]{:S(2)}) async-start(f32[64,1,512]{2,1,0:T(1,128)} %dynamic-slice_bitcast_fusion.3), calls=%async_computation | async-start | bytes 262144 | tf_op jit(solution)/shard_map/all_to_all | solution.py:54
Sparse Core Ops, SparseCore 0:
  27.8 777.7 all-reduce.2
  810.8 30.0 all-gather.11
  842.7 35.0 all-gather.13
  879.5 34.5 all-gather.15
  915.7 31.8 all-gather.9
